TPU v7x, 512 devices: a whole 4x4x16 slice. The times are simulated.
512 devices in a mesh: tm: 32 (over z, core), band: 4 (over y), fsdp: 4 (over x).
Axes of the slice: x: 4, y: 4, z: 16, core: 2. Of those that a mesh axis runs over, the one named last changes fastest.
Arguments:
- video: bfloat16 [128, 64, 128, 256], P('tm', 'band', 'fsdp'), may hold values from -8 to 8
- clip_lengths: int32 [16], replicated, may hold values from 1 to 31, 128 in all
- norm_gains: float32 [2, 256], replicated, may hold values from 0.1 to 1.9
- spatial_kernel_weight: bfloat16 [256, 2304], P(('band', 'fsdp')), may hold values from -0.125 to 0.125
- w_time: bfloat16 [256, 768], P(('band', 'fsdp')), may hold values from -0.21875 to 0.21875
- w_qkv: bfloat16 [256, 768], P(('band', 'fsdp')), may hold values from -4 to 4
- w_out: bfloat16 [256, 256], P(('band', 'fsdp')), may hold values from -0.375 to 0.375
Outputs:
- mixed: bfloat16 [4, 4, 512, 128, 256], P('band', 'fsdp', 'tm')
Inputs may be any that keep to these rules, and one draw needn't show every extreme that they name: `clip_lengths`: every clip has at least one frame and the lengths sum to 128.
All inputs are finite; a program needn't handle non-finite values.
Results may differ from a plain program's by a relative error of at most 0.0064.
Values may be sent and summed in bfloat16 or wider, within the bound.
No kernel may reach another device: no remote copies, remote signals or barrier semaphores. Data moves between devices by JAX's collectives and lax.ppermute only.
A program may use at most 64 MiB of HBM per device.

v0:
```python
import math
import jax
import jax.numpy as jnp
from jax import lax
from jax.sharding import PartitionSpec as P

GROUPS = 32
EPS = 1e-06


def with_halo(x, sides, width):
    for axis, dim in sides:
        size, length = (lax.axis_size(axis), x.shape[dim])
        up = [(i, (i + 1) % size) for i in range(size - 1)]
        down = [(j, i) for i, j in up]
        last = lax.slice_in_dim(x, length - width, length, axis=dim)
        initial = lax.slice_in_dim(x, 0, width, axis=dim)
        before = lax.ppermute(last, axis, up)
        after = lax.ppermute(initial, axis, down)
        x = jnp.concatenate([before, x, after], axis=dim)
    return x


def from_behind(x, axis, by):
    length = lax.axis_size(axis)
    pairs = [(i, i + by) for i in range(length) if 0 <= i + by < length]
    return lax.ppermute(x, axis, pairs)


def butterfly_sum(x, axes):
    for axis in axes:
        size = lax.axis_size(axis)
        step = 1
        while step < size:
            pairs = [(i, i ^ step) for i in range(size)]
            x = x + lax.ppermute(x, axis, pairs)
            step *= 2
    return x


def frame_starts(clip_lengths, total):
    ends = jnp.cumsum(clip_lengths)
    begins = ends - clip_lengths
    index = jnp.arange(total, dtype=jnp.int32)
    chosen = jnp.where(begins[None, :] <= index[:, None], begins[None, :], 0)
    return jnp.max(chosen, axis=1)


def group_moments(field):
    frames, height, width, chans = field.shape
    group_width = chans // GROUPS
    vals = field.astype(jnp.float32).reshape(frames, height * width, GROUPS, group_width)
    sums = jnp.sum(vals, axis=(1, 3))
    squares = jnp.sum(vals * vals, axis=(1, 3))
    both = butterfly_sum(jnp.stack([sums, squares]), ("band", "fsdp"))
    sums, squares = (both[0], both[1])
    count = height * width * group_width * lax.axis_size("band") * lax.axis_size("fsdp")
    mean = sums / count
    scale = lax.rsqrt(squares / count - mean * mean + EPS)
    return (mean, scale)


def apply_norm(field, mean, scale, gain):
    shape = field.shape
    chans = shape[-1]
    group_width = chans // GROUPS
    vals = field.astype(jnp.float32).reshape(shape[0], -1, GROUPS, group_width)
    normed = (vals - mean[:, None, :, None]) * scale[:, None, :, None]
    return normed.reshape(shape) * gain


def body(video, clip_lengths, norm_gains, spatial_kernel_weight, w_time, w_qkv, w_out):
    frames, height, width, chans = video.shape
    widths = [w.shape[1] for w in (spatial_kernel_weight, w_time, w_qkv, w_out)]
    packed = jnp.concatenate([spatial_kernel_weight, w_time, w_qkv, w_out], axis=1)
    gathered = lax.all_gather(packed, ("band", "fsdp"), axis=0, tiled=True)
    offsets = [sum(widths[:i]) for i in range(4)]
    space_full, time_full, qkv_full, output_complete = [
        gathered[:, o : o + w] for o, w in zip(offsets, widths)
    ]
    ranks = lax.axis_size("tm")
    total_frames = frames * ranks
    first = lax.axis_index("tm") * frames
    starts = frame_starts(clip_lengths, total_frames)
    local_starts = lax.dynamic_slice_in_dim(starts, first, frames)
    mean_one, scale_one = group_moments(video)
    act = jax.nn.silu(apply_norm(video, mean_one, scale_one, norm_gains[0])).astype(jnp.bfloat16)
    padded = with_halo(act, (("band", 1), ("fsdp", 2)), 1)
    spatial = jnp.zeros((frames, height, width, chans), jnp.float32)
    for tap in range(9):
        shift_y = tap // 3
        shift_x = tap % 3
        spatial = spatial + jnp.einsum(
            "fhwc,cd->fhwd",
            padded[:, shift_y : shift_y + height, shift_x : shift_x + width],
            space_full[:, tap * chans : (tap + 1) * chans],
            preferred_element_type=jnp.float32,
        )
    spatial = spatial.astype(jnp.bfloat16)
    carried = from_behind(spatial[frames - 2 :], "tm", 1)
    extended = jnp.concatenate([carried, spatial], axis=0)
    position = first + jnp.arange(frames, dtype=jnp.int32)
    slots = jnp.arange(frames + 2, dtype=jnp.int32)
    temporal = jnp.zeros((frames, height, width, chans), jnp.float32)
    for tap in range(3):
        source = jnp.maximum(position - 2 + tap, local_starts) - first + 2
        select = (source[:, None] == slots[None, :]).astype(jnp.bfloat16)
        picked = jnp.einsum(
            "fe,ehwc->fhwc", select, extended, preferred_element_type=jnp.float32
        ).astype(jnp.bfloat16)
        temporal = temporal + jnp.einsum(
            "fhwc,cd->fhwd",
            picked,
            time_full[:, tap * chans : (tap + 1) * chans],
            preferred_element_type=jnp.float32,
        )
    resid = (video.astype(jnp.float32) + temporal).astype(jnp.bfloat16)
    pixels = height * width
    group_pixels = pixels // ranks
    flat_resid = resid.reshape(frames, ranks, group_pixels, chans).transpose(1, 0, 2, 3)
    received = lax.all_to_all(flat_resid, "tm", split_axis=0, concat_axis=0, tiled=True)
    resid_time = received.reshape(total_frames, group_pixels, chans)
    mean_two, scale_two = group_moments(resid)
    mine = jnp.concatenate([mean_two, scale_two], axis=1)
    big = jnp.pad(mine, ((0, 8 - frames), (0, 1024 - 2 * GROUPS)))
    moments = lax.all_gather(big, "tm", axis=0, tiled=True).reshape(ranks, 8, 1024)[
        :, :frames, : 2 * GROUPS
    ]
    moments = moments.reshape(total_frames, 2 * GROUPS)
    mean_all, scale_all = (moments[:, :GROUPS], moments[:, GROUPS:])
    flat_norm = apply_norm(resid_time, mean_all, scale_all, norm_gains[1]).astype(jnp.bfloat16)
    qkv_time = jnp.einsum(
        "fpc,cd->fpd", flat_norm, qkv_full, preferred_element_type=jnp.float32
    ).astype(jnp.bfloat16)
    query = qkv_time[..., :chans]
    keys = qkv_time[..., chans : 2 * chans]
    value_rows = qkv_time[..., 2 * chans :]
    index = jnp.arange(total_frames, dtype=jnp.int32)
    allowed = (index[None, :] <= index[:, None]) & (index[None, :] >= starts[:, None])
    scores = jnp.einsum(
        "fpc,gpc->pfg", query, keys, preferred_element_type=jnp.float32
    ) / math.sqrt(chans)
    scores = jnp.where(allowed[None], scores, -1e30)
    top = jnp.max(scores, axis=-1, keepdims=True)
    expo = jnp.where(allowed[None], jnp.exp(scores - top), 0.0)
    attention_probabilities = (expo / jnp.sum(expo, axis=-1, keepdims=True)).astype(jnp.bfloat16)
    attention_output = jnp.einsum(
        "boh,hba->boa", attention_probabilities, value_rows, preferred_element_type=jnp.float32
    ).astype(jnp.bfloat16)
    projected_output = jnp.einsum(
        "axi,iy->axy", attention_output, output_complete, preferred_element_type=jnp.float32
    )
    mixed = (jnp.swapaxes(resid_time, 0, 1).astype(jnp.float32) + projected_output).astype(
        jnp.bfloat16
    )
    return mixed.reshape(1, 1, mixed.shape[0], total_frames, chans)


def solution(mesh):
    return jax.shard_map(
        body,
        mesh=mesh,
        in_specs=(
            P("tm", "band", "fsdp", None),
            P(),
            P(),
            P(("band", "fsdp"), None),
            P(("band", "fsdp"), None),
            P(("band", "fsdp"), None),
            P(("band", "fsdp"), None),
        ),
        out_specs=P("band", "fsdp", "tm", None, None),
        check_vma=False,
    )
```

profile of v0, /device:TPU:1, one launch (start us, length us, event | category | flops | bytes accessed | tf_op | source)
XLA Modules:
  0.0 233.3 jit_solution(3845554850148898094)
XLA Ops:
  6.5 1.7 pad_maximum_fusion.2
  8.3 1.5 convert_reduce_fusion
  10.2 4.0 %collective-permute-start = (f32[2,4,32]{2,1,0:T(4,128)S(1)}, f32[2,4,32]{2,1,0:T(4,128)S(1)}, u32[]{:S(2)}, u32[]{:S(2)}) collective-permute-start(f32[2,4,32]{2,1,0:T(4,128)S(1)} %pad_maximum_fusion.6), channel_id=1, source_target_pairs={{0,4},{4,0},{8,12},{12,8},{1,5},{5,1},{9,13},{13,9},{2,6},{6,2},{1... | collective-permute-start | bytes 3080 | tf_op jit(solution)/shard_map/ppermute | solution.py:36
  15.2 5.0 %collective-permute-start.1 = (f32[2,4,32]{2,1,0:T(4,128)S(1)}, f32[2,4,32]{2,1,0:T(4,128)S(1)}, u32[]{:S(2)}, u32[]{:S(2)}) collective-permute-start(f32[2,4,32]{2,1,0:T(4,128)S(1)} %fusion.93), channel_id=1, source_target_pairs={{0,8},{4,12},{8,0},{12,4},{1,9},{5,13},{9,1},{13,5},{2,10},{6,14},... | collective-permute-start | bytes 3080 | tf_op jit(solution)/shard_map/ppermute | solution.py:36
  21.2 3.2 %collective-permute-start.2 = (f32[2,4,32]{2,1,0:T(4,128)S(1)}, f32[2,4,32]{2,1,0:T(4,128)S(1)}, u32[]{:S(2)}, u32[]{:S(2)}) collective-permute-start(f32[2,4,32]{2,1,0:T(4,128)S(1)} %fusion.104), channel_id=1, source_target_pairs={{0,1},{1,0},{2,3},{3,2},{4,5},{5,4},{6,7},{7,6},{8,9},{9,8},{10,11... | collective-permute-start | bytes 3080 | tf_op jit(solution)/shard_map/ppermute | solution.py:36
  25.5 4.7 %collective-permute-start.3 = (f32[2,4,32]{2,1,0:T(4,128)S(1)}, f32[2,4,32]{2,1,0:T(4,128)S(1)}, u32[]{:S(2)}, u32[]{:S(2)}) collective-permute-start(f32[2,4,32]{2,1,0:T(4,128)S(1)} %add.111), channel_id=1, source_target_pairs={{0,2},{1,3},{2,0},{3,1},{4,6},{5,7},{6,4},{7,5},{8,10},{9,11},{10,... | collective-permute-start | bytes 3080 | tf_op jit(solution)/shard_map/ppermute | solution.py:36
  32.4 3.2 %collective-permute-start.4 = (bf16[4,1,32,256]{3,2,1,0:T(8,128)(2,1)S(1)}, bf16[4,1,32,256]{3,2,1,0:T(8,128)(2,1)S(1)}, u32[]{:S(2)}, u32[]{:S(2)}) collective-permute-start(bf16[4,1,32,256]{3,2,1,0:T(8,128)(2,1)S(1)} %get-tuple-element.13), channel_id=1, source_target_pairs={{0,4},{4,8},{8,12},{1,5},{5,9},{9,13},{2,6},{6,10},{10,14},{3,7},{... | collective-permute-start | bytes 196616 | tf_op jit(solution)/shard_map/ppermute | solution.py:18
  35.7 1.3 collective-permute-start.5
  37.0 4.1 %collective-permute-done.5 = bf16[4,1,32,256]{3,2,1,0:T(8,128)(2,1)S(1)} collective-permute-done((bf16[4,1,32,256]{3,2,1,0:T(8,128)(2,1)S(1)}, bf16[4,1,32,256]{3,2,1,0:T(8,128)(2,1)S(1)}, u32[]{:S(2)}, u32[]{:S(2)}) %collective-permute-start.5) | collective-permute-done | bytes 65568 | tf_op jit(solution)/shard_map/ppermute | solution.py:19
  41.3 3.2 %collective-permute-start.6 = (bf16[4,18,1,256]{3,2,1,0:T(2,128)(2,1)S(1)}, bf16[4,18,1,256]{3,2,1,0:T(2,128)(2,1)S(1)}, u32[]{:S(2)}, u32[]{:S(2)}) collective-permute-start(bf16[4,18,1,256]{3,2,1,0:T(2,128)(2,1)S(1)} %get-tuple-element.12), channel_id=1, source_target_pairs={{0,1},{1,2},{2,3},{4,5},{5,6},{6,7},{8,9},{9,10},{10,11},{12,13},{... | collective-permute-start | bytes 110600 | tf_op jit(solution)/shard_map/ppermute | solution.py:18
  45.9 3.7 %collective-permute-done.7 = bf16[4,18,1,256]{3,2,1,0:T(2,128)(2,1)S(1)} collective-permute-done((bf16[4,18,1,256]{3,2,1,0:T(2,128)(2,1)S(1)}, bf16[4,18,1,256]{3,2,1,0:T(2,128)(2,1)S(1)}, u32[]{:S(2)}, u32[]{:S(2)}) %collective-permute-start.7) | collective-permute-done | bytes 36896 | tf_op jit(solution)/shard_map/ppermute | solution.py:19
  49.6 1.8 pad_maximum_fusion.1
  51.3 23.3 %all-gather.3.cloned.1.call-done = bf16[256,4096]{1,0:T(8,128)(2,1)} async-done(((bf16[16,4096]{1,0:T(8,128)(2,1)}), bf16[256,4096]{1,0:T(8,128)(2,1)}) %all-gather.3.cloned.1.call-update) | async-done | bytes 2097168 | tf_op jit(solution)/shard_map/all_gather | solution.py:76
  74.7 1.5 fusion.51
  81.5 5.3 %collective-permute-start.8 = (bf16[2,16,32,256]{3,2,1,0:T(8,128)(2,1)S(1)}, bf16[2,16,32,256]{3,2,1,0:T(8,128)(2,1)S(1)}, u32[]{:S(2)}, u32[]{:S(2)}) collective-permute-start(bf16[2,16,32,256]{3,2,1,0:T(8,128)(2,1)S(1)} %slice.197), channel_id=1, source_target_pairs={{0,16},{16,32},{32,48},{48,64},{64,80},{80,96},{96,112},{112,128},... | collective-permute-start | bytes 1572872 | tf_op jit(solution)/shard_map/ppermute | solution.py:27
  87.2 5.7 %collective-permute-done.8 = bf16[2,16,32,256]{3,2,1,0:T(8,128)(2,1)S(1)} collective-permute-done((bf16[2,16,32,256]{3,2,1,0:T(8,128)(2,1)S(1)}, bf16[2,16,32,256]{3,2,1,0:T(8,128)(2,1)S(1)}, u32[]{:S(2)}, u32[]{:S(2)}) %collective-permute-start.8) | collective-permute-done | bytes 524320 | tf_op jit(solution)/shard_map/ppermute | solution.py:27
  96.6 1.3 fusion.60
  98.0 1.4 fusion.62
  99.4 1.7 convert_reduce_fusion.1
  102.3 15.1 %all-to-all-start = ((bf16[32,4,16,256]{3,2,1,0:T(8,128)(2,1)}), bf16[32,4,16,256]{3,2,1,0:T(8,128)(2,1)S(1)}, u32[]{:S(2)}, u32[]{:S(2)}) async-start(bf16[32,4,16,256]{3,2,1,0:T(8,128)(2,1)} %bitcast.135), calls=%async_computation | async-start | bytes 2097152 | tf_op jit(solution)/shard_map/all_to_all | solution.py:121
  117.8 2.8 %collective-permute-start.9 = (f32[2,4,32]{2,1,0:T(4,128)S(1)}, f32[2,4,32]{2,1,0:T(4,128)S(1)}, u32[]{:S(2)}, u32[]{:S(2)}) collective-permute-start(f32[2,4,32]{2,1,0:T(4,128)S(1)} %pad_maximum_fusion.7), channel_id=1, source_target_pairs={{0,4},{4,0},{8,12},{12,8},{1,5},{5,1},{9,13},{13,9},{2,6},{6,2},{1... | collective-permute-start | bytes 3080 | tf_op jit(solution)/shard_map/ppermute | solution.py:36
  120.6 1.8 collective-permute-done.9
  122.5 3.7 %collective-permute-start.10 = (f32[2,4,32]{2,1,0:T(4,128)S(1)}, f32[2,4,32]{2,1,0:T(4,128)S(1)}, u32[]{:S(2)}, u32[]{:S(2)}) collective-permute-start(f32[2,4,32]{2,1,0:T(4,128)S(1)} %fusion.92), channel_id=1, source_target_pairs={{0,8},{4,12},{8,0},{12,4},{1,9},{5,13},{9,1},{13,5},{2,10},{6,14},... | collective-permute-start | bytes 3080 | tf_op jit(solution)/shard_map/ppermute | solution.py:36
  126.2 2.4 %collective-permute-done.10 = f32[2,4,32]{2,1,0:T(4,128)S(1)} collective-permute-done((f32[2,4,32]{2,1,0:T(4,128)S(1)}, f32[2,4,32]{2,1,0:T(4,128)S(1)}, u32[]{:S(2)}, u32[]{:S(2)}) %collective-permute-start.10) | collective-permute-done | bytes 1056 | tf_op jit(solution)/shard_map/ppermute | solution.py:36
  128.6 2.8 %collective-permute-start.11 = (f32[2,4,32]{2,1,0:T(4,128)S(1)}, f32[2,4,32]{2,1,0:T(4,128)S(1)}, u32[]{:S(2)}, u32[]{:S(2)}) collective-permute-start(f32[2,4,32]{2,1,0:T(4,128)S(1)} %fusion.103), channel_id=1, source_target_pairs={{0,1},{1,0},{2,3},{3,2},{4,5},{5,4},{6,7},{7,6},{8,9},{9,8},{10,11... | collective-permute-start | bytes 3080 | tf_op jit(solution)/shard_map/ppermute | solution.py:36
  131.4 1.8 collective-permute-done.11
  133.2 3.7 %collective-permute-start.12 = (f32[2,4,32]{2,1,0:T(4,128)S(1)}, f32[2,4,32]{2,1,0:T(4,128)S(1)}, u32[]{:S(2)}, u32[]{:S(2)}) collective-permute-start(f32[2,4,32]{2,1,0:T(4,128)S(1)} %add.132), channel_id=1, source_target_pairs={{0,2},{1,3},{2,0},{3,1},{4,6},{5,7},{6,4},{7,5},{8,10},{9,11},{10,... | collective-permute-start | bytes 3080 | tf_op jit(solution)/shard_map/ppermute | solution.py:36
  137.0 2.4 %collective-permute-done.12 = f32[2,4,32]{2,1,0:T(4,128)S(1)} collective-permute-done((f32[2,4,32]{2,1,0:T(4,128)S(1)}, f32[2,4,32]{2,1,0:T(4,128)S(1)}, u32[]{:S(2)}, u32[]{:S(2)}) %collective-permute-start.12) | collective-permute-done | bytes 1056 | tf_op jit(solution)/shard_map/ppermute | solution.py:36
  140.1 73.9 %all-gather.5.cloned.1.call-done = f32[256,1024]{1,0:T(8,128)} async-done(((f32[8,1024]{1,0:T(8,128)}), f32[256,1024]{1,0:T(8,128)}) %all-gather.5.cloned.1.call-update) | async-done | bytes 1048592 | tf_op jit(solution)/shard_map/all_gather | solution.py:126
  215.8 4.6 %convolution_convert_fusion = bf16[128,16,768]{2,0,1:T(8,128)(2,1)} fusion(f32[128,16,256]{2,1,0:T(8,128)S(1)} %bitcast_convert_fusion, f32[256]{0:T(256)S(1)} %bitcast.150, f32[128,256]{1,0:T(8,128)S(1)} %copy.42, f32[128,256]{1,0:T(8,128)S(1)} %copy.40, bf16[256,4096]{1,0:T(8,128)(2,1)} %all-gather.3.cloned.1.call-done), kind=kOutput, calls=%fused_computation.7 | convolution fusion | flops 808976384 | bytes 5899264 | tf_op jit(solution)/shard_map/fpc,cd->fpd/dot_general | solution.py:132
  220.4 2.1 fusion.97
  222.5 3.9 %fusion.31 = bf16[1,1,16,128,256]{4,3,2,1,0:T(8,128)(2,1)} fusion(f32[128,16,256]{2,1,0:T(8,128)S(1)} %bitcast_convert_fusion, bf16[128,16,768]{2,0,1:T(8,128)(2,1)} %convolution_convert_fusion, f32[16,128,128]{1,2,0:T(8,128)S(1)} %get-tuple-element.24, f32[16,128]{1,0:T(8,128)S(1)} %get-tuple-element.23, bf16[256,4096]{1,0:T(8,128)(2,1)} %all-gather.3.cloned.1.call-done), kind=kOutput, calls=%fused_computation.39 | convolution fusion | flops 404750336 | bytes 5382144 | tf_op jit(solution)/shard_map/axi,iy->axy/dot_general | solution.py:150
  (83 shorter events, 20.7 us)
Async XLA Ops:
  6.5 25.2 %copy-start.1 = (bf16[4,16,32,256]{3,2,1,0:T(8,128)(2,1)S(1)}, bf16[4,16,32,256]{3,2,1,0:T(8,128)(2,1)}, u32[]{:S(2)}) copy-start(bf16[4,16,32,256]{3,2,1,0:T(8,128)(2,1)} %param.7) | copy-start | bytes 3145732
  6.5 68.1 %all-gather.3.cloned.1.call-start = ((), (), s32[]{:S(2)}) async-start(), calls=%async_computation.1 | async-start | bytes 2228224 | tf_op jit(solution)/shard_map/all_gather | solution.py:76
  10.2 5.0 %collective-permute-start = (f32[2,4,32]{2,1,0:T(4,128)S(1)}, f32[2,4,32]{2,1,0:T(4,128)S(1)}, u32[]{:S(2)}, u32[]{:S(2)}) collective-permute-start(f32[2,4,32]{2,1,0:T(4,128)S(1)} %pad_maximum_fusion.6), channel_id=1, source_target_pairs={{0,4},{4,0},{8,12},{12,8},{1,5},{5,1},{9,13},{13,9},{2,6},{6,2},{1... | collective-permute-start | bytes 3080 | tf_op jit(solution)/shard_map/ppermute | solution.py:36
  15.2 6.0 %collective-permute-start.1 = (f32[2,4,32]{2,1,0:T(4,128)S(1)}, f32[2,4,32]{2,1,0:T(4,128)S(1)}, u32[]{:S(2)}, u32[]{:S(2)}) collective-permute-start(f32[2,4,32]{2,1,0:T(4,128)S(1)} %fusion.93), channel_id=1, source_target_pairs={{0,8},{4,12},{8,0},{12,4},{1,9},{5,13},{9,1},{13,5},{2,10},{6,14},... | collective-permute-start | bytes 3080 | tf_op jit(solution)/shard_map/ppermute | solution.py:36
  21.2 4.3 %collective-permute-start.2 = (f32[2,4,32]{2,1,0:T(4,128)S(1)}, f32[2,4,32]{2,1,0:T(4,128)S(1)}, u32[]{:S(2)}, u32[]{:S(2)}) collective-permute-start(f32[2,4,32]{2,1,0:T(4,128)S(1)} %fusion.104), channel_id=1, source_target_pairs={{0,1},{1,0},{2,3},{3,2},{4,5},{5,4},{6,7},{7,6},{8,9},{9,8},{10,11... | collective-permute-start | bytes 3080 | tf_op jit(solution)/shard_map/ppermute | solution.py:36
  25.5 5.8 %collective-permute-start.3 = (f32[2,4,32]{2,1,0:T(4,128)S(1)}, f32[2,4,32]{2,1,0:T(4,128)S(1)}, u32[]{:S(2)}, u32[]{:S(2)}) collective-permute-start(f32[2,4,32]{2,1,0:T(4,128)S(1)} %add.111), channel_id=1, source_target_pairs={{0,2},{1,3},{2,0},{3,1},{4,6},{5,7},{6,4},{7,5},{8,10},{9,11},{10,... | collective-permute-start | bytes 3080 | tf_op jit(solution)/shard_map/ppermute | solution.py:36
  32.4 4.6 %collective-permute-start.4 = (bf16[4,1,32,256]{3,2,1,0:T(8,128)(2,1)S(1)}, bf16[4,1,32,256]{3,2,1,0:T(8,128)(2,1)S(1)}, u32[]{:S(2)}, u32[]{:S(2)}) collective-permute-start(bf16[4,1,32,256]{3,2,1,0:T(8,128)(2,1)S(1)} %get-tuple-element.13), channel_id=1, source_target_pairs={{0,4},{4,8},{8,12},{1,5},{5,9},{9,13},{2,6},{6,10},{10,14},{3,7},{... | collective-permute-start | bytes 196616 | tf_op jit(solution)/shard_map/ppermute | solution.py:18
  35.7 5.4 %collective-permute-start.5 = (bf16[4,1,32,256]{3,2,1,0:T(8,128)(2,1)S(1)}, bf16[4,1,32,256]{3,2,1,0:T(8,128)(2,1)S(1)}, u32[]{:S(2)}, u32[]{:S(2)}) collective-permute-start(bf16[4,1,32,256]{3,2,1,0:T(8,128)(2,1)S(1)} %get-tuple-element.14), channel_id=1, source_target_pairs={{4,0},{8,4},{12,8},{5,1},{9,5},{13,9},{6,2},{10,6},{14,10},{7,3},{... | collective-permute-start | bytes 196616 | tf_op jit(solution)/shard_map/ppermute | solution.py:19
  41.3 4.6 %collective-permute-start.6 = (bf16[4,18,1,256]{3,2,1,0:T(2,128)(2,1)S(1)}, bf16[4,18,1,256]{3,2,1,0:T(2,128)(2,1)S(1)}, u32[]{:S(2)}, u32[]{:S(2)}) collective-permute-start(bf16[4,18,1,256]{3,2,1,0:T(2,128)(2,1)S(1)} %get-tuple-element.12), channel_id=1, source_target_pairs={{0,1},{1,2},{2,3},{4,5},{5,6},{6,7},{8,9},{9,10},{10,11},{12,13},{... | collective-permute-start | bytes 110600 | tf_op jit(solution)/shard_map/ppermute | solution.py:18
  44.5 5.1 %collective-permute-start.7 = (bf16[4,18,1,256]{3,2,1,0:T(2,128)(2,1)S(1)}, bf16[4,18,1,256]{3,2,1,0:T(2,128)(2,1)S(1)}, u32[]{:S(2)}, u32[]{:S(2)}) collective-permute-start(bf16[4,18,1,256]{3,2,1,0:T(2,128)(2,1)S(1)} %get-tuple-element.11), channel_id=1, source_target_pairs={{1,0},{2,1},{3,2},{5,4},{6,5},{7,6},{9,8},{10,9},{11,10},{13,12},{... | collective-permute-start | bytes 110600 | tf_op jit(solution)/shard_map/ppermute | solution.py:19
  74.6 1.7 copy-start.3
  76.3 1.4 copy-start
  80.4 6.4 %copy-start.4 = (s32[16]{0:T(128)S(1)}, s32[16]{0:T(128)}, u32[]{:S(2)}) copy-start(s32[16]{0:T(128)} %param.8) | copy-start | bytes 196
  81.5 11.4 %collective-permute-start.8 = (bf16[2,16,32,256]{3,2,1,0:T(8,128)(2,1)S(1)}, bf16[2,16,32,256]{3,2,1,0:T(8,128)(2,1)S(1)}, u32[]{:S(2)}, u32[]{:S(2)}) collective-permute-start(bf16[2,16,32,256]{3,2,1,0:T(8,128)(2,1)S(1)} %slice.197), channel_id=1, source_target_pairs={{0,16},{16,32},{32,48},{48,64},{64,80},{80,96},{96,112},{112,128},... | collective-permute-start | bytes 1572872 | tf_op jit(solution)/shard_map/ppermute | solution.py:27
  98.0 1.4 copy-start.2
  102.3 113.1 %all-to-all-start = ((bf16[32,4,16,256]{3,2,1,0:T(8,128)(2,1)}), bf16[32,4,16,256]{3,2,1,0:T(8,128)(2,1)S(1)}, u32[]{:S(2)}, u32[]{:S(2)}) async-start(bf16[32,4,16,256]{3,2,1,0:T(8,128)(2,1)} %bitcast.135), calls=%async_computation | async-start | bytes 2097152 | tf_op jit(solution)/shard_map/all_to_all | solution.py:121
  117.4 96.7 %all-gather.5.cloned.1.call-start = ((), (), s32[]{:S(2)}) async-start(), calls=%async_computation.2 | async-start | bytes 1081344 | tf_op jit(solution)/shard_map/all_gather | solution.py:126
  117.8 4.6 %collective-permute-start.9 = (f32[2,4,32]{2,1,0:T(4,128)S(1)}, f32[2,4,32]{2,1,0:T(4,128)S(1)}, u32[]{:S(2)}, u32[]{:S(2)}) collective-permute-start(f32[2,4,32]{2,1,0:T(4,128)S(1)} %pad_maximum_fusion.7), channel_id=1, source_target_pairs={{0,4},{4,0},{8,12},{12,8},{1,5},{5,1},{9,13},{13,9},{2,6},{6,2},{1... | collective-permute-start | bytes 3080 | tf_op jit(solution)/shard_map/ppermute | solution.py:36
  122.5 6.1 %collective-permute-start.10 = (f32[2,4,32]{2,1,0:T(4,128)S(1)}, f32[2,4,32]{2,1,0:T(4,128)S(1)}, u32[]{:S(2)}, u32[]{:S(2)}) collective-permute-start(f32[2,4,32]{2,1,0:T(4,128)S(1)} %fusion.92), channel_id=1, source_target_pairs={{0,8},{4,12},{8,0},{12,4},{1,9},{5,13},{9,1},{13,5},{2,10},{6,14},... | collective-permute-start | bytes 3080 | tf_op jit(solution)/shard_map/ppermute | solution.py:36
  128.6 4.6 %collective-permute-start.11 = (f32[2,4,32]{2,1,0:T(4,128)S(1)}, f32[2,4,32]{2,1,0:T(4,128)S(1)}, u32[]{:S(2)}, u32[]{:S(2)}) collective-permute-start(f32[2,4,32]{2,1,0:T(4,128)S(1)} %fusion.103), channel_id=1, source_target_pairs={{0,1},{1,0},{2,3},{3,2},{4,5},{5,4},{6,7},{7,6},{8,9},{9,8},{10,11... | collective-permute-start | bytes 3080 | tf_op jit(solution)/shard_map/ppermute | solution.py:36
  133.2 6.1 %collective-permute-start.12 = (f32[2,4,32]{2,1,0:T(4,128)S(1)}, f32[2,4,32]{2,1,0:T(4,128)S(1)}, u32[]{:S(2)}, u32[]{:S(2)}) collective-permute-start(f32[2,4,32]{2,1,0:T(4,128)S(1)} %add.132), channel_id=1, source_target_pairs={{0,2},{1,3},{2,0},{3,1},{4,6},{5,7},{6,4},{7,5},{8,10},{9,11},{10,... | collective-permute-start | bytes 3080 | tf_op jit(solution)/shard_map/ppermute | solution.py:36
Sparse Core Ops, SparseCore 0:
  10.3 64.2 all-gather.2
  140.2 73.7 all-gather.4
where the time goes:
time: 234 us; the launch traced here: 233 us
  waiting for transfers between devices  123 us (53%)
  starting transfers between devices  59.3 us (25%)
  matrix products  24.5 us (10%)
  between operations  13.8 us (6%)
  other arithmetic  7.72 us (3%)
  local copies, waits for them, and re-layouts  5.18 us (2%)
    all_gather x1, waiting for transfers between devices, body(): lax.all_gather(big, 'tm', axis=0, tiled=True).reshape(ranks, 8, 1024)  73.9 us
    ppermute x8, starting transfers between devices, butterfly_sum(): x = x + lax.ppermute(x, axis, pairs)  29.9 us
    all_gather x1, waiting for transfers between devices, body(): gathered = lax.all_gather(packed, ('band', 'fsdp'), axis=0, tiled=True)  23.3 us
    all_to_all x1, starting transfers between devices, body(): lax.all_to_all(flat_resid, 'tm', split_axis=0, concat_axis=0, tiled=True)  15.1 us
    ppermute x8, waiting for transfers between devices, butterfly_sum(): x = x + lax.ppermute(x, axis, pairs)  12 us
    ppermute x2, waiting for transfers between devices, with_halo(): after = lax.ppermute(initial, axis, down)  7.84 us
    ppermute x2, starting transfers between devices, with_halo(): before = lax.ppermute(last, axis, up)  6.45 us
    dot_general x9, matrix products, body(): jnp.einsum('fhwc,cd->fhwd', padded[:, shift_y:shift_y + height, shift_x:s...  5.7 us
  transfers between devices with their start and end apart: 16, of which 14 were waited for; matrix products, arithmetic and copies ran while one was open for 4% of the time, Pallas kernels for 0%

commit v1 on v0

--- a/solution.py
+++ b/solution.py
@@ -6,6 +6,12 @@
 
 GROUPS = 32
 EPS = 1e-06
+
+
+def chains_create(buf, which_dim):
+    val = list(buf.shape[1:])
+    val[which_dim] *= buf.shape[0]
+    return jnp.moveaxis(buf, 0, which_dim).reshape(val)
 
 
 def with_halo(x, sides, width):
@@ -73,7 +79,31 @@
     frames, height, width, chans = video.shape
     widths = [w.shape[1] for w in (spatial_kernel_weight, w_time, w_qkv, w_out)]
     packed = jnp.concatenate([spatial_kernel_weight, w_time, w_qkv, w_out], axis=1)
-    gathered = lax.all_gather(packed, ("band", "fsdp"), axis=0, tiled=True)
+    heap = []
+    k_all = lax.axis_size(("band", "fsdp"))
+    b = 0
+    while b < k_all:
+        heap.append((b, (b + 1) % k_all))
+        b = b + 1
+    buffers = []
+    for j0, dev_j in heap:
+        buffers.append((dev_j, j0))
+    current_arr, built = ([], [])
+    no = 0
+    while no < k_all - 1:
+        if no % 2 == 0:
+            current_arr.append(
+                lax.ppermute(
+                    current_arr[-1] if current_arr else packed, ("band", "fsdp"), perm=heap
+                )
+            )
+        else:
+            built.append(lax.ppermute(built[-1] if built else packed, ("band", "fsdp"), buffers))
+        no = no + 1
+    fresh = jnp.stack([*current_arr[::-1], packed, *built], axis=0)
+    val2 = lax.axis_index(("band", "fsdp")) - len(current_arr)
+    fresh = fresh[(jnp.arange(k_all) - val2) % k_all]
+    gathered = chains_create(fresh, 0)
     offsets = [sum(widths[:i]) for i in range(4)]
     space_full, time_full, qkv_full, output_complete = [
         gathered[:, o : o + w] for o, w in zip(offsets, widths)

time: 234 us -> 293 us (1.25)
  starting transfers between devices: 59.3 us -> 120 us
  waiting for transfers between devices: 123 us -> 98.3 us
  local copies, waits for them, and re-layouts: 5.18 us -> 21.3 us
  matrix products: 24.5 us -> 31.8 us
    ppermute x0 -> x15, starting transfers between devices: none -> 60.9 us  [the longest x7 44.4 us: body(): lax.ppermute(built[-1] if built else packed, ('band', 'fsdp'), buffers)]
    all_gather x1 -> x0, waiting for transfers between devices: 23.3 us -> none  [body(): gathered = lax.all_gather(packed, ('band', 'fsdp'), axis=0, tiled=True)]
    unnamed x12 -> x32, local copies, waits for them, and re-layouts: 1.2 us -> 12.4 us
    ppermute x8, starting transfers between devices: 29.9 us -> 21.2 us  [butterfly_sum(): x = x + lax.ppermute(x, axis, pairs)]
    ppermute x2, waiting for transfers between devices: 7.84 us -> 0.01 us  [with_halo(): after = lax.ppermute(initial, axis, down)]
    dot_general x9, matrix products: 5.7 us -> 13.2 us  [body(): jnp.einsum('fhwc,cd->fhwd', padded[:, shift_y:shift_y + height, shift_x:s...]
    ppermute x1, starting transfers between devices: 5.27 us -> 12.2 us  [from_behind(): return lax.ppermute(x, axis, pairs)]
    ppermute x0 -> x15, waiting for transfers between devices: none -> 5.85 us  [the longest x8 5.83 us: body(): lax.ppermute(current_arr[-1] if current_arr else packed, ('band', 'fsdp')...]
  transfers between devices with their start and end apart: 16 -> 30, of which waited for: 14 -> 11; matrix products, arithmetic and copies ran while one was open for 4% -> 7% of each run, Pallas kernels for 0% -> 0%
where the time goes in v1:
time: 293 us; the launch traced here: 291 us
  starting transfers between devices  120 us (41%)
  waiting for transfers between devices  98.3 us (34%)
  matrix products  31.8 us (11%)
  local copies, waits for them, and re-layouts  21.3 us (7%)
  between operations  14.1 us (5%)
  other arithmetic  6.17 us (2%)
    all_gather x1, waiting for transfers between devices, body(): lax.all_gather(big, 'tm', axis=0, tiled=True).reshape(ranks, 8, 1024)  71.9 us
    ppermute x7, starting transfers between devices, body(): lax.ppermute(built[-1] if built else packed, ('band', 'fsdp'), buffers)  44.4 us
    ppermute x8, starting transfers between devices, butterfly_sum(): x = x + lax.ppermute(x, axis, pairs)  21.2 us
    all_to_all x1, starting transfers between devices, body(): lax.all_to_all(flat_resid, 'tm', split_axis=0, concat_axis=0, tiled=True)  17.4 us
    ppermute x8, starting transfers between devices, body(): lax.ppermute(current_arr[-1] if current_arr else packed, ('band', 'fsdp')...  16.5 us
    ppermute x8, waiting for transfers between devices, butterfly_sum(): x = x + lax.ppermute(x, axis, pairs)  15.1 us
    dot_general x9, matrix products, body(): jnp.einsum('fhwc,cd->fhwd', padded[:, shift_y:shift_y + height, shift_x:s...  13.2 us
    unnamed x32, local copies, waits for them, and re-layouts  12.4 us
  transfers between devices with their start and end apart: 30, of which 11 were waited for; matrix products, arithmetic and copies ran while one was open for 7% of the time, Pallas kernels for 0%

profile of v1, /device:TPU:1, one launch (start us, length us, event | category | flops | bytes accessed | tf_op | source)
XLA Modules:
  0.0 291.3 jit_solution(13787952974042604179)
XLA Ops:
  8.5 4.0 %collective-permute-start = (f32[2,4,32]{2,1,0:T(4,128)S(1)}, f32[2,4,32]{2,1,0:T(4,128)S(1)}, u32[]{:S(2)}, u32[]{:S(2)}) collective-permute-start(f32[2,4,32]{2,1,0:T(4,128)S(1)} %pad_maximum_fusion.5), channel_id=1, source_target_pairs={{0,4},{4,0},{8,12},{12,8},{1,5},{5,1},{9,13},{13,9},{2,6},{6,2},{1... | collective-permute-start | bytes 3080 | tf_op jit(solution)/shard_map/ppermute | solution.py:42
  15.0 4.5 %collective-permute-start.1 = (f32[2,4,32]{2,1,0:T(4,128)S(1)}, f32[2,4,32]{2,1,0:T(4,128)S(1)}, u32[]{:S(2)}, u32[]{:S(2)}) collective-permute-start(f32[2,4,32]{2,1,0:T(4,128)S(1)} %fusion.95), channel_id=1, source_target_pairs={{0,8},{4,12},{8,0},{12,4},{1,9},{5,13},{9,1},{13,5},{2,10},{6,14},... | collective-permute-start | bytes 3080 | tf_op jit(solution)/shard_map/ppermute | solution.py:42
  20.2 3.1 %collective-permute-start.7 = (bf16[16,4096]{1,0:T(8,128)(2,1)S(1)}, bf16[16,4096]{1,0:T(8,128)(2,1)S(1)}, u32[]{:S(2)}, u32[]{:S(2)}) collective-permute-start(bf16[16,4096]{1,0:T(8,128)(2,1)S(1)} %constant_dynamic-update-slice_fusion), channel_id=1, source_target_pairs={{0,1},{1,2},{2,3},{3,4},{4,5},{5,6},{6,7},{7,8},{8,9},{9,10},{10,1... | collective-permute-start | bytes 393224 | tf_op jit(solution)/shard_map/ppermute | solution.py:96
  23.3 3.1 %collective-permute-start.2 = (f32[2,4,32]{2,1,0:T(4,128)S(1)}, f32[2,4,32]{2,1,0:T(4,128)S(1)}, u32[]{:S(2)}, u32[]{:S(2)}) collective-permute-start(f32[2,4,32]{2,1,0:T(4,128)S(1)} %fusion.106), channel_id=1, source_target_pairs={{0,1},{1,0},{2,3},{3,2},{4,5},{5,4},{6,7},{7,6},{8,9},{9,8},{10,11... | collective-permute-start | bytes 3080 | tf_op jit(solution)/shard_map/ppermute | solution.py:42
  26.5 4.3 %collective-permute-start.15 = (bf16[16,4096]{1,0:T(8,128)(2,1)S(1)}, bf16[16,4096]{1,0:T(8,128)(2,1)S(1)}, u32[]{:S(2)}, u32[]{:S(2)}) collective-permute-start(bf16[16,4096]{1,0:T(8,128)(2,1)S(1)} %constant_dynamic-update-slice_fusion), channel_id=1, source_target_pairs={{1,0},{2,1},{3,2},{4,3},{5,4},{6,5},{7,6},{8,7},{9,8},{10,9},{11,1... | collective-permute-start | bytes 393224 | tf_op jit(solution)/shard_map/ppermute | solution.py:101
  30.8 1.9 collective-permute-start.3
  32.7 1.9 collective-permute-start.8
  36.6 5.1 %collective-permute-done.8 = bf16[16,4096]{1,0:T(8,128)(2,1)S(1)} collective-permute-done((bf16[16,4096]{1,0:T(8,128)(2,1)S(1)}, bf16[16,4096]{1,0:T(8,128)(2,1)S(1)}, u32[]{:S(2)}, u32[]{:S(2)}) %collective-permute-start.8) | collective-permute-done | bytes 131104 | tf_op jit(solution)/shard_map/ppermute | solution.py:96
  43.9 6.7 %collective-permute-start.16 = (bf16[16,4096]{1,0:T(8,128)(2,1)S(1)}, bf16[16,4096]{1,0:T(8,128)(2,1)S(1)}, u32[]{:S(2)}, u32[]{:S(2)}) collective-permute-start(bf16[16,4096]{1,0:T(8,128)(2,1)S(1)} %collective-permute-done.15), channel_id=1, source_target_pairs={{1,0},{2,1},{3,2},{4,3},{5,4},{6,5},{7,6},{8,7},{9,8},{10,9},{11,1... | collective-permute-start | bytes 393224 | tf_op jit(solution)/shard_map/ppermute | solution.py:101
  50.8 1.9 collective-permute-start.10
  52.9 6.7 %collective-permute-start.17 = (bf16[16,4096]{1,0:T(8,128)(2,1)S(1)}, bf16[16,4096]{1,0:T(8,128)(2,1)S(1)}, u32[]{:S(2)}, u32[]{:S(2)}) collective-permute-start(bf16[16,4096]{1,0:T(8,128)(2,1)S(1)} %collective-permute-done.16), channel_id=1, source_target_pairs={{1,0},{2,1},{3,2},{4,3},{5,4},{6,5},{7,6},{8,7},{9,8},{10,9},{11,1... | collective-permute-start | bytes 393224 | tf_op jit(solution)/shard_map/ppermute | solution.py:101
  62.4 6.7 %collective-permute-start.18 = (bf16[16,4096]{1,0:T(8,128)(2,1)S(1)}, bf16[16,4096]{1,0:T(8,128)(2,1)S(1)}, u32[]{:S(2)}, u32[]{:S(2)}) collective-permute-start(bf16[16,4096]{1,0:T(8,128)(2,1)S(1)} %collective-permute-done.17), channel_id=1, source_target_pairs={{1,0},{2,1},{3,2},{4,3},{5,4},{6,5},{7,6},{8,7},{9,8},{10,9},{11,1... | collective-permute-start | bytes 393224 | tf_op jit(solution)/shard_map/ppermute | solution.py:101
  73.9 9.4 %collective-permute-start.19 = (bf16[16,4096]{1,0:T(8,128)(2,1)S(1)}, bf16[16,4096]{1,0:T(8,128)(2,1)S(1)}, u32[]{:S(2)}, u32[]{:S(2)}) collective-permute-start(bf16[16,4096]{1,0:T(8,128)(2,1)S(1)} %collective-permute-done.18), channel_id=1, source_target_pairs={{1,0},{2,1},{3,2},{4,3},{5,4},{6,5},{7,6},{8,7},{9,8},{10,9},{11,1... | collective-permute-start | bytes 393224 | tf_op jit(solution)/shard_map/ppermute | solution.py:101
  83.3 1.9 collective-permute-start.13
  86.7 4.0 %collective-permute-start.6 = (bf16[4,18,1,256]{3,2,1,0:T(2,128)(2,1)S(1)}, bf16[4,18,1,256]{3,2,1,0:T(2,128)(2,1)S(1)}, u32[]{:S(2)}, u32[]{:S(2)}) collective-permute-start(bf16[4,18,1,256]{3,2,1,0:T(2,128)(2,1)S(1)} %get-tuple-element.12), channel_id=1, source_target_pairs={{0,1},{1,2},{2,3},{4,5},{5,6},{6,7},{8,9},{9,10},{10,11},{12,13},{... | collective-permute-start | bytes 110600 | tf_op jit(solution)/shard_map/ppermute | solution.py:24
  90.7 4.0 %collective-permute-start.20 = (bf16[16,4096]{1,0:T(8,128)(2,1)S(1)}, bf16[16,4096]{1,0:T(8,128)(2,1)S(1)}, u32[]{:S(2)}, u32[]{:S(2)}) collective-permute-start(bf16[16,4096]{1,0:T(8,128)(2,1)S(1)} %collective-permute-done.19), channel_id=1, source_target_pairs={{1,0},{2,1},{3,2},{4,3},{5,4},{6,5},{7,6},{8,7},{9,8},{10,9},{11,1... | collective-permute-start | bytes 393224 | tf_op jit(solution)/shard_map/ppermute | solution.py:101
  94.7 1.9 collective-permute-start.14
  98.5 6.7 %collective-permute-start.21 = (bf16[16,4096]{1,0:T(8,128)(2,1)S(1)}, bf16[16,4096]{1,0:T(8,128)(2,1)S(1)}, u32[]{:S(2)}, u32[]{:S(2)}) collective-permute-start(bf16[16,4096]{1,0:T(8,128)(2,1)S(1)} %collective-permute-done.20), channel_id=1, source_target_pairs={{1,0},{2,1},{3,2},{4,3},{5,4},{6,5},{7,6},{8,7},{9,8},{10,9},{11,1... | collective-permute-start | bytes 393224 | tf_op jit(solution)/shard_map/ppermute | solution.py:101
  115.7 3.6 %gather_fusion = bf16[16,16,4096]{2,1,0:T(8,128)(2,1)} fusion(bf16[16,16,4096]{2,1,0:T(8,128)(2,1)} %bitcast_dynamic-update-slice_fusion, s32[1024]{0:T(1024)S(1)} %pad_clamp_fusion), kind=kCustom, calls=%fused_computation | custom fusion | bytes 4194368 | tf_op jit(solution)/shard_map/gather | solution.py:105
  130.6 2.0 add_convert_fusion
  132.6 12.2 %collective-permute-start.23 = (bf16[2,16,32,256]{3,2,1,0:T(8,128)(2,1)S(1)}, bf16[2,16,32,256]{3,2,1,0:T(8,128)(2,1)S(1)}, u32[]{:S(2)}, u32[]{:S(2)}) collective-permute-start(bf16[2,16,32,256]{3,2,1,0:T(8,128)(2,1)S(1)} %slice.199), channel_id=1, source_target_pairs={{0,16},{16,32},{32,48},{48,64},{64,80},{80,96},{96,112},{112,128},... | collective-permute-start | bytes 1572872 | tf_op jit(solution)/shard_map/ppermute | solution.py:33
  145.3 5.5 %collective-permute-done.23 = bf16[2,16,32,256]{3,2,1,0:T(8,128)(2,1)S(1)} collective-permute-done((bf16[2,16,32,256]{3,2,1,0:T(8,128)(2,1)S(1)}, bf16[2,16,32,256]{3,2,1,0:T(8,128)(2,1)S(1)}, u32[]{:S(2)}, u32[]{:S(2)}) %collective-permute-start.23) | collective-permute-done | bytes 524320 | tf_op jit(solution)/shard_map/ppermute | solution.py:33
  160.1 17.4 %all-to-all-start = ((bf16[32,4,16,256]{3,2,1,0:T(8,128)(2,1)}), bf16[32,4,16,256]{3,2,1,0:T(8,128)(2,1)S(1)}, u32[]{:S(2)}, u32[]{:S(2)}) async-start(bf16[32,4,16,256]{3,2,1,0:T(8,128)(2,1)} %bitcast.170), calls=%async_computation | async-start | bytes 2097152 | tf_op jit(solution)/shard_map/all_to_all | solution.py:151
  177.9 1.9 collective-permute-start.24
  179.9 2.7 collective-permute-done.24
  184.5 4.2 %collective-permute-done.25 = f32[2,4,32]{2,1,0:T(4,128)S(1)} collective-permute-done((f32[2,4,32]{2,1,0:T(4,128)S(1)}, f32[2,4,32]{2,1,0:T(4,128)S(1)}, u32[]{:S(2)}, u32[]{:S(2)}) %collective-permute-start.25) | collective-permute-done | bytes 1056 | tf_op jit(solution)/shard_map/ppermute | solution.py:42
  190.6 2.7 collective-permute-done.26
  195.3 4.2 %collective-permute-done.27 = f32[2,4,32]{2,1,0:T(4,128)S(1)} collective-permute-done((f32[2,4,32]{2,1,0:T(4,128)S(1)}, f32[2,4,32]{2,1,0:T(4,128)S(1)}, u32[]{:S(2)}, u32[]{:S(2)}) %collective-permute-start.27) | collective-permute-done | bytes 1056 | tf_op jit(solution)/shard_map/ppermute | solution.py:42
  200.3 71.9 %all-gather.2.cloned.1.call-done = f32[256,1024]{1,0:T(8,128)} async-done(((f32[8,1024]{1,0:T(8,128)}), f32[256,1024]{1,0:T(8,128)}) %all-gather.2.cloned.1.call-update) | async-done | bytes 1048592 | tf_op jit(solution)/shard_map/all_gather | solution.py:156
  273.9 4.6 %convolution_convert_fusion = bf16[128,16,768]{2,0,1:T(8,128)(2,1)} fusion(f32[128,16,256]{2,1,0:T(8,128)S(1)} %bitcast_convert_fusion, f32[256]{0:T(256)S(1)} %bitcast.199, f32[128,256]{1,0:T(8,128)S(1)} %copy.42, f32[128,256]{1,0:T(8,128)S(1)} %copy.40, bf16[256,4096]{1,0:T(8,128)(2,1)} %bitcast.183), kind=kOutput, calls=%fused_computation.8 | convolution fusion | flops 808976384 | bytes 5899264 | tf_op jit(solution)/shard_map/fpc,cd->fpd/dot_general | solution.py:162
  278.5 2.1 fusion.99
  280.6 3.9 %fusion.31 = bf16[1,1,16,128,256]{4,3,2,1,0:T(8,128)(2,1)} fusion(f32[128,16,256]{2,1,0:T(8,128)S(1)} %bitcast_convert_fusion, bf16[128,16,768]{2,0,1:T(8,128)(2,1)} %convolution_convert_fusion, f32[16,128,128]{1,2,0:T(8,128)S(1)} %get-tuple-element.24, f32[16,128]{1,0:T(8,128)S(1)} %get-tuple-element.23, bf16[256,4096]{1,0:T(8,128)(2,1)} %bitcast.184), kind=kOutput, calls=%fused_computation.40 | convolution fusion | flops 404750336 | bytes 5382144 | tf_op jit(solution)/shard_map/axi,iy->axy/dot_general | solution.py:180
  (134 shorter events, 60.4 us)
Async XLA Ops:
  6.5 55.2 %copy-start.1 = (bf16[4,16,32,256]{3,2,1,0:T(8,128)(2,1)S(1)}, bf16[4,16,32,256]{3,2,1,0:T(8,128)(2,1)}, u32[]{:S(2)}) copy-start(bf16[4,16,32,256]{3,2,1,0:T(8,128)(2,1)} %param.7) | copy-start | bytes 3145732
  8.5 6.4 %collective-permute-start = (f32[2,4,32]{2,1,0:T(4,128)S(1)}, f32[2,4,32]{2,1,0:T(4,128)S(1)}, u32[]{:S(2)}, u32[]{:S(2)}) collective-permute-start(f32[2,4,32]{2,1,0:T(4,128)S(1)} %pad_maximum_fusion.5), channel_id=1, source_target_pairs={{0,4},{4,0},{8,12},{12,8},{1,5},{5,1},{9,13},{13,9},{2,6},{6,2},{1... | collective-permute-start | bytes 3080 | tf_op jit(solution)/shard_map/ppermute | solution.py:42
  15.0 8.4 %collective-permute-start.1 = (f32[2,4,32]{2,1,0:T(4,128)S(1)}, f32[2,4,32]{2,1,0:T(4,128)S(1)}, u32[]{:S(2)}, u32[]{:S(2)}) collective-permute-start(f32[2,4,32]{2,1,0:T(4,128)S(1)} %fusion.95), channel_id=1, source_target_pairs={{0,8},{4,12},{8,0},{12,4},{1,9},{5,13},{9,1},{13,5},{2,10},{6,14},... | collective-permute-start | bytes 3080 | tf_op jit(solution)/shard_map/ppermute | solution.py:42
  20.2 12.5 %collective-permute-start.7 = (bf16[16,4096]{1,0:T(8,128)(2,1)S(1)}, bf16[16,4096]{1,0:T(8,128)(2,1)S(1)}, u32[]{:S(2)}, u32[]{:S(2)}) collective-permute-start(bf16[16,4096]{1,0:T(8,128)(2,1)S(1)} %constant_dynamic-update-slice_fusion), channel_id=1, source_target_pairs={{0,1},{1,2},{2,3},{3,4},{4,5},{5,6},{6,7},{7,8},{8,9},{9,10},{10,1... | collective-permute-start | bytes 393224 | tf_op jit(solution)/shard_map/ppermute | solution.py:96
  23.3 7.4 %collective-permute-start.2 = (f32[2,4,32]{2,1,0:T(4,128)S(1)}, f32[2,4,32]{2,1,0:T(4,128)S(1)}, u32[]{:S(2)}, u32[]{:S(2)}) collective-permute-start(f32[2,4,32]{2,1,0:T(4,128)S(1)} %fusion.106), channel_id=1, source_target_pairs={{0,1},{1,0},{2,3},{3,2},{4,5},{5,4},{6,7},{7,6},{8,9},{9,8},{10,11... | collective-permute-start | bytes 3080 | tf_op jit(solution)/shard_map/ppermute | solution.py:42
  26.5 17.4 %collective-permute-start.15 = (bf16[16,4096]{1,0:T(8,128)(2,1)S(1)}, bf16[16,4096]{1,0:T(8,128)(2,1)S(1)}, u32[]{:S(2)}, u32[]{:S(2)}) collective-permute-start(bf16[16,4096]{1,0:T(8,128)(2,1)S(1)} %constant_dynamic-update-slice_fusion), channel_id=1, source_target_pairs={{1,0},{2,1},{3,2},{4,3},{5,4},{6,5},{7,6},{8,7},{9,8},{10,9},{11,1... | collective-permute-start | bytes 393224 | tf_op jit(solution)/shard_map/ppermute | solution.py:101
  30.8 5.9 %collective-permute-start.3 = (f32[2,4,32]{2,1,0:T(4,128)S(1)}, f32[2,4,32]{2,1,0:T(4,128)S(1)}, u32[]{:S(2)}, u32[]{:S(2)}) collective-permute-start(f32[2,4,32]{2,1,0:T(4,128)S(1)} %add.138), channel_id=1, source_target_pairs={{0,2},{1,3},{2,0},{3,1},{4,6},{5,7},{6,4},{7,5},{8,10},{9,11},{10,... | collective-permute-start | bytes 3080 | tf_op jit(solution)/shard_map/ppermute | solution.py:42
  32.7 9.0 %collective-permute-start.8 = (bf16[16,4096]{1,0:T(8,128)(2,1)S(1)}, bf16[16,4096]{1,0:T(8,128)(2,1)S(1)}, u32[]{:S(2)}, u32[]{:S(2)}) collective-permute-start(bf16[16,4096]{1,0:T(8,128)(2,1)S(1)} %collective-permute-done.7), channel_id=1, source_target_pairs={{0,1},{1,2},{2,3},{3,4},{4,5},{5,6},{6,7},{7,8},{8,9},{9,10},{10,1... | collective-permute-start | bytes 393224 | tf_op jit(solution)/shard_map/ppermute | solution.py:96
  41.7 9.0 %collective-permute-start.9 = (bf16[16,4096]{1,0:T(8,128)(2,1)S(1)}, bf16[16,4096]{1,0:T(8,128)(2,1)S(1)}, u32[]{:S(2)}, u32[]{:S(2)}) collective-permute-start(bf16[16,4096]{1,0:T(8,128)(2,1)S(1)} %collective-permute-done.8), channel_id=1, source_target_pairs={{0,1},{1,2},{2,3},{3,4},{4,5},{5,6},{6,7},{7,8},{8,9},{9,10},{10,1... | collective-permute-start | bytes 393224 | tf_op jit(solution)/shard_map/ppermute | solution.py:96
  43.9 9.0 %collective-permute-start.16 = (bf16[16,4096]{1,0:T(8,128)(2,1)S(1)}, bf16[16,4096]{1,0:T(8,128)(2,1)S(1)}, u32[]{:S(2)}, u32[]{:S(2)}) collective-permute-start(bf16[16,4096]{1,0:T(8,128)(2,1)S(1)} %collective-permute-done.15), channel_id=1, source_target_pairs={{1,0},{2,1},{3,2},{4,3},{5,4},{6,5},{7,6},{8,7},{9,8},{10,9},{11,1... | collective-permute-start | bytes 393224 | tf_op jit(solution)/shard_map/ppermute | solution.py:101
  50.8 9.0 %collective-permute-start.10 = (bf16[16,4096]{1,0:T(8,128)(2,1)S(1)}, bf16[16,4096]{1,0:T(8,128)(2,1)S(1)}, u32[]{:S(2)}, u32[]{:S(2)}) collective-permute-start(bf16[16,4096]{1,0:T(8,128)(2,1)S(1)} %collective-permute-done.9), channel_id=1, source_target_pairs={{0,1},{1,2},{2,3},{3,4},{4,5},{5,6},{6,7},{7,8},{8,9},{9,10},{10,1... | collective-permute-start | bytes 393224 | tf_op jit(solution)/shard_map/ppermute | solution.py:96
  52.9 9.5 %collective-permute-start.17 = (bf16[16,4096]{1,0:T(8,128)(2,1)S(1)}, bf16[16,4096]{1,0:T(8,128)(2,1)S(1)}, u32[]{:S(2)}, u32[]{:S(2)}) collective-permute-start(bf16[16,4096]{1,0:T(8,128)(2,1)S(1)} %collective-permute-done.16), channel_id=1, source_target_pairs={{1,0},{2,1},{3,2},{4,3},{5,4},{6,5},{7,6},{8,7},{9,8},{10,9},{11,1... | collective-permute-start | bytes 393224 | tf_op jit(solution)/shard_map/ppermute | solution.py:101
  59.8 36.9 %copy-start.3 = (bf16[16,4096]{1,0:T(8,128)(2,1)}, bf16[16,4096]{1,0:T(8,128)(2,1)S(1)}, u32[]{:S(2)}) copy-start(bf16[16,4096]{1,0:T(8,128)(2,1)S(1)} %collective-permute-done.10) | copy-start | bytes 393220
  59.8 9.6 %collective-permute-start.11 = (bf16[16,4096]{1,0:T(8,128)(2,1)S(1)}, bf16[16,4096]{1,0:T(8,128)(2,1)S(1)}, u32[]{:S(2)}, u32[]{:S(2)}) collective-permute-start(bf16[16,4096]{1,0:T(8,128)(2,1)S(1)} %collective-permute-done.10), channel_id=1, source_target_pairs={{0,1},{1,2},{2,3},{3,4},{4,5},{5,6},{6,7},{7,8},{8,9},{9,10},{10,1... | collective-permute-start | bytes 393224 | tf_op jit(solution)/shard_map/ppermute | solution.py:96
  62.4 11.5 %collective-permute-start.18 = (bf16[16,4096]{1,0:T(8,128)(2,1)S(1)}, bf16[16,4096]{1,0:T(8,128)(2,1)S(1)}, u32[]{:S(2)}, u32[]{:S(2)}) collective-permute-start(bf16[16,4096]{1,0:T(8,128)(2,1)S(1)} %collective-permute-done.17), channel_id=1, source_target_pairs={{1,0},{2,1},{3,2},{4,3},{5,4},{6,5},{7,6},{8,7},{9,8},{10,9},{11,1... | collective-permute-start | bytes 393224 | tf_op jit(solution)/shard_map/ppermute | solution.py:101
  69.4 14.0 %collective-permute-start.12 = (bf16[16,4096]{1,0:T(8,128)(2,1)S(1)}, bf16[16,4096]{1,0:T(8,128)(2,1)S(1)}, u32[]{:S(2)}, u32[]{:S(2)}) collective-permute-start(bf16[16,4096]{1,0:T(8,128)(2,1)S(1)} %collective-permute-done.11), channel_id=1, source_target_pairs={{0,1},{1,2},{2,3},{3,4},{4,5},{5,6},{6,7},{7,8},{8,9},{9,10},{10,1... | collective-permute-start | bytes 393224 | tf_op jit(solution)/shard_map/ppermute | solution.py:96
  71.3 14.0 %collective-permute-start.4 = (bf16[4,1,32,256]{3,2,1,0:T(8,128)(2,1)S(1)}, bf16[4,1,32,256]{3,2,1,0:T(8,128)(2,1)S(1)}, u32[]{:S(2)}, u32[]{:S(2)}) collective-permute-start(bf16[4,1,32,256]{3,2,1,0:T(8,128)(2,1)S(1)} %get-tuple-element.13), channel_id=1, source_target_pairs={{0,4},{4,8},{8,12},{1,5},{5,9},{9,13},{2,6},{6,10},{10,14},{3,7},{... | collective-permute-start | bytes 196616 | tf_op jit(solution)/shard_map/ppermute | solution.py:24
  72.6 12.7 %collective-permute-start.5 = (bf16[4,1,32,256]{3,2,1,0:T(8,128)(2,1)S(1)}, bf16[4,1,32,256]{3,2,1,0:T(8,128)(2,1)S(1)}, u32[]{:S(2)}, u32[]{:S(2)}) collective-permute-start(bf16[4,1,32,256]{3,2,1,0:T(8,128)(2,1)S(1)} %get-tuple-element.14), channel_id=1, source_target_pairs={{4,0},{8,4},{12,8},{5,1},{9,5},{13,9},{6,2},{10,6},{14,10},{7,3},{... | collective-permute-start | bytes 196616 | tf_op jit(solution)/shard_map/ppermute | solution.py:25
  73.9 16.8 %collective-permute-start.19 = (bf16[16,4096]{1,0:T(8,128)(2,1)S(1)}, bf16[16,4096]{1,0:T(8,128)(2,1)S(1)}, u32[]{:S(2)}, u32[]{:S(2)}) collective-permute-start(bf16[16,4096]{1,0:T(8,128)(2,1)S(1)} %collective-permute-done.18), channel_id=1, source_target_pairs={{1,0},{2,1},{3,2},{4,3},{5,4},{6,5},{7,6},{8,7},{9,8},{10,9},{11,1... | collective-permute-start | bytes 393224 | tf_op jit(solution)/shard_map/ppermute | solution.py:101
  83.3 11.4 %collective-permute-start.13 = (bf16[16,4096]{1,0:T(8,128)(2,1)S(1)}, bf16[16,4096]{1,0:T(8,128)(2,1)S(1)}, u32[]{:S(2)}, u32[]{:S(2)}) collective-permute-start(bf16[16,4096]{1,0:T(8,128)(2,1)S(1)} %collective-permute-done.12), channel_id=1, source_target_pairs={{0,1},{1,2},{2,3},{3,4},{4,5},{5,6},{6,7},{7,8},{8,9},{9,10},{10,1... | collective-permute-start | bytes 393224 | tf_op jit(solution)/shard_map/ppermute | solution.py:96
  85.4 11.3 %collective-permute-start.22 = (bf16[4,18,1,256]{3,2,1,0:T(2,128)(2,1)S(1)}, bf16[4,18,1,256]{3,2,1,0:T(2,128)(2,1)S(1)}, u32[]{:S(2)}, u32[]{:S(2)}) collective-permute-start(bf16[4,18,1,256]{3,2,1,0:T(2,128)(2,1)S(1)} %get-tuple-element.11), channel_id=1, source_target_pairs={{1,0},{2,1},{3,2},{5,4},{6,5},{7,6},{9,8},{10,9},{11,10},{13,12},{... | collective-permute-start | bytes 110600 | tf_op jit(solution)/shard_map/ppermute | solution.py:25
  86.7 10.0 %collective-permute-start.6 = (bf16[4,18,1,256]{3,2,1,0:T(2,128)(2,1)S(1)}, bf16[4,18,1,256]{3,2,1,0:T(2,128)(2,1)S(1)}, u32[]{:S(2)}, u32[]{:S(2)}) collective-permute-start(bf16[4,18,1,256]{3,2,1,0:T(2,128)(2,1)S(1)} %get-tuple-element.12), channel_id=1, source_target_pairs={{0,1},{1,2},{2,3},{4,5},{5,6},{6,7},{8,9},{9,10},{10,11},{12,13},{... | collective-permute-start | bytes 110600 | tf_op jit(solution)/shard_map/ppermute | solution.py:24
  90.7 7.8 %collective-permute-start.20 = (bf16[16,4096]{1,0:T(8,128)(2,1)S(1)}, bf16[16,4096]{1,0:T(8,128)(2,1)S(1)}, u32[]{:S(2)}, u32[]{:S(2)}) collective-permute-start(bf16[16,4096]{1,0:T(8,128)(2,1)S(1)} %collective-permute-done.19), channel_id=1, source_target_pairs={{1,0},{2,1},{3,2},{4,3},{5,4},{6,5},{7,6},{8,7},{9,8},{10,9},{11,1... | collective-permute-start | bytes 393224 | tf_op jit(solution)/shard_map/ppermute | solution.py:101
  94.7 10.4 %collective-permute-start.14 = (bf16[16,4096]{1,0:T(8,128)(2,1)S(1)}, bf16[16,4096]{1,0:T(8,128)(2,1)S(1)}, u32[]{:S(2)}, u32[]{:S(2)}) collective-permute-start(bf16[16,4096]{1,0:T(8,128)(2,1)S(1)} %collective-permute-done.13), channel_id=1, source_target_pairs={{0,1},{1,2},{2,3},{3,4},{4,5},{5,6},{6,7},{7,8},{8,9},{9,10},{10,1... | collective-permute-start | bytes 393224 | tf_op jit(solution)/shard_map/ppermute | solution.py:96
  98.5 16.6 %collective-permute-start.21 = (bf16[16,4096]{1,0:T(8,128)(2,1)S(1)}, bf16[16,4096]{1,0:T(8,128)(2,1)S(1)}, u32[]{:S(2)}, u32[]{:S(2)}) collective-permute-start(bf16[16,4096]{1,0:T(8,128)(2,1)S(1)} %collective-permute-done.20), channel_id=1, source_target_pairs={{1,0},{2,1},{3,2},{4,3},{5,4},{6,5},{7,6},{8,7},{9,8},{10,9},{11,1... | collective-permute-start | bytes 393224 | tf_op jit(solution)/shard_map/ppermute | solution.py:101
  132.6 18.1 %collective-permute-start.23 = (bf16[2,16,32,256]{3,2,1,0:T(8,128)(2,1)S(1)}, bf16[2,16,32,256]{3,2,1,0:T(8,128)(2,1)S(1)}, u32[]{:S(2)}, u32[]{:S(2)}) collective-permute-start(bf16[2,16,32,256]{3,2,1,0:T(8,128)(2,1)S(1)} %slice.199), channel_id=1, source_target_pairs={{0,16},{16,32},{32,48},{48,64},{64,80},{80,96},{96,112},{112,128},... | collective-permute-start | bytes 1572872 | tf_op jit(solution)/shard_map/ppermute | solution.py:33
  160.1 113.5 %all-to-all-start = ((bf16[32,4,16,256]{3,2,1,0:T(8,128)(2,1)}), bf16[32,4,16,256]{3,2,1,0:T(8,128)(2,1)S(1)}, u32[]{:S(2)}, u32[]{:S(2)}) async-start(bf16[32,4,16,256]{3,2,1,0:T(8,128)(2,1)} %bitcast.170), calls=%async_computation | async-start | bytes 2097152 | tf_op jit(solution)/shard_map/all_to_all | solution.py:151
  177.5 94.7 %all-gather.2.cloned.1.call-start = ((), (), s32[]{:S(2)}) async-start(), calls=%async_computation.1 | async-start | bytes 1081344 | tf_op jit(solution)/shard_map/all_gather | solution.py:156
  177.9 4.6 %collective-permute-start.24 = (f32[2,4,32]{2,1,0:T(4,128)S(1)}, f32[2,4,32]{2,1,0:T(4,128)S(1)}, u32[]{:S(2)}, u32[]{:S(2)}) collective-permute-start(f32[2,4,32]{2,1,0:T(4,128)S(1)} %pad_maximum_fusion.6), channel_id=1, source_target_pairs={{0,4},{4,0},{8,12},{12,8},{1,5},{5,1},{9,13},{13,9},{2,6},{6,2},{1... | collective-permute-start | bytes 3080 | tf_op jit(solution)/shard_map/ppermute | solution.py:42
  182.6 6.1 %collective-permute-start.25 = (f32[2,4,32]{2,1,0:T(4,128)S(1)}, f32[2,4,32]{2,1,0:T(4,128)S(1)}, u32[]{:S(2)}, u32[]{:S(2)}) collective-permute-start(f32[2,4,32]{2,1,0:T(4,128)S(1)} %fusion.94), channel_id=1, source_target_pairs={{0,8},{4,12},{8,0},{12,4},{1,9},{5,13},{9,1},{13,5},{2,10},{6,14},... | collective-permute-start | bytes 3080 | tf_op jit(solution)/shard_map/ppermute | solution.py:42
  188.7 4.6 %collective-permute-start.26 = (f32[2,4,32]{2,1,0:T(4,128)S(1)}, f32[2,4,32]{2,1,0:T(4,128)S(1)}, u32[]{:S(2)}, u32[]{:S(2)}) collective-permute-start(f32[2,4,32]{2,1,0:T(4,128)S(1)} %fusion.105), channel_id=1, source_target_pairs={{0,1},{1,0},{2,3},{3,2},{4,5},{5,4},{6,7},{7,6},{8,9},{9,8},{10,11... | collective-permute-start | bytes 3080 | tf_op jit(solution)/shard_map/ppermute | solution.py:42
  193.4 6.1 %collective-permute-start.27 = (f32[2,4,32]{2,1,0:T(4,128)S(1)}, f32[2,4,32]{2,1,0:T(4,128)S(1)}, u32[]{:S(2)}, u32[]{:S(2)}) collective-permute-start(f32[2,4,32]{2,1,0:T(4,128)S(1)} %add.162), channel_id=1, source_target_pairs={{0,2},{1,3},{2,0},{3,1},{4,6},{5,7},{6,4},{7,5},{8,10},{9,11},{10,... | collective-permute-start | bytes 3080 | tf_op jit(solution)/shard_map/ppermute | solution.py:42
  (4 other events, 28.5 us)
Sparse Core Ops, SparseCore 0:
  200.4 71.7 all-gather.1
